TPU v7x, 32 devices: a whole 2x2x4 slice. The times are simulated.
32 devices in a mesh: section: 2 (over x), dp: 4 (over z), mp: 4 (over y, core).
Axes of the slice: x: 2, y: 2, z: 4, core: 2. Of those that a mesh axis runs over, the one named last changes fastest.
Arguments:
- queries: bfloat16 [2, 4, 640, 4096], P('section', 'dp', None, 'mp')
- keys: bfloat16 [2, 4, 640, 4096], P('section', 'dp', None, 'mp')
- values: bfloat16 [2, 4, 640, 4096], P('section', 'dp', None, 'mp'), may hold values from -6 to 6
- grad_out: bfloat16 [2, 4, 640, 4096], P('section', 'dp', None, 'mp'), may hold values from -6 to 6
- positions: int32 [2, 4, 640], P('section', 'dp'), may hold values from 0 to 319, as said below
Outputs:
- received: bfloat16 [2, 4, 3, 640, 4096], P('section', 'dp', None, 'mp')
- bias_grad: float32 [2, 3, 4096], P('section')
Inputs may be any that keep to these rules, and one draw needn't show every extreme that they name: `positions`: along each sequence a position is 0 or one more than the position before it; the first is 0; a document starts at token 320, and none is longer than 320 tokens.
All inputs are finite; a program needn't handle non-finite values.
Results may differ from a plain program's by a relative error of at most 0.0065.
Values may be sent and summed in bfloat16 or wider, within the bound.
No kernel may reach another device: no remote copies, remote signals or barrier semaphores. Data moves between devices by JAX's collectives and lax.ppermute only.
A program may use at most 64 MiB of HBM per device.

v0:
```python
import math
import jax
import jax.numpy as jnp
from jax import lax
from jax.sharding import PartitionSpec as P

HEAD_DIM = 128


def from_behind(value, axis, steps):
    count = lax.axis_size(axis)
    initial, last = (max(0, -steps), min(count, count - steps))
    return lax.ppermute(value, axis, [(source, source + steps) for source in range(initial, last)])


def per_device(queries, keys, values, grad_out, positions):
    query_rows = queries[0, 0]
    key_rows = keys[0, 0]
    value_rows = values[0, 0]
    grad_rows = grad_out[0, 0]
    token_positions = positions[0, 0]
    length = query_rows.shape[0]
    columns = query_rows.shape[1]
    head_count = columns // HEAD_DIM
    scaling = 1.0 / math.sqrt(HEAD_DIM)
    indices = jnp.arange(length, dtype=jnp.int32)
    allowed = (indices[None, :] <= indices[:, None]) & (
        indices[None, :] >= (indices - token_positions)[:, None]
    )

    def one_head(head, results):
        offset = head * HEAD_DIM
        query_part = lax.dynamic_slice_in_dim(query_rows, offset, HEAD_DIM, 1)
        key_part = lax.dynamic_slice_in_dim(key_rows, offset, HEAD_DIM, 1)
        value_part = lax.dynamic_slice_in_dim(value_rows, offset, HEAD_DIM, 1)
        grad_part = lax.dynamic_slice_in_dim(grad_rows, offset, HEAD_DIM, 1)
        scores = (
            jnp.einsum("qd,kd->qk", query_part, key_part, preferred_element_type=jnp.float32)
            * scaling
        )
        scores = jnp.where(allowed, scores, jnp.float32(-1e30))
        highest = jnp.max(scores, axis=-1, keepdims=True)
        expont = jnp.exp(scores - highest)
        attn = expont / jnp.sum(expont, axis=-1, keepdims=True)
        attn_low = attn.astype(jnp.bfloat16)
        grad_v = jnp.einsum("qk,qd->kd", attn_low, grad_part, preferred_element_type=jnp.float32)
        grad_attn = jnp.einsum(
            "qd,kd->qk", grad_part, value_part, preferred_element_type=jnp.float32
        )
        delta = jnp.sum(attn * grad_attn, axis=-1, keepdims=True)
        grad_scores = (attn * (grad_attn - delta) * scaling).astype(jnp.bfloat16)
        grad_q = jnp.einsum("qk,kd->qd", grad_scores, key_part, preferred_element_type=jnp.float32)
        grad_k = jnp.einsum(
            "qk,qd->kd", grad_scores, query_part, preferred_element_type=jnp.float32
        )
        blocks = jnp.stack([grad_q, grad_k, grad_v]).astype(jnp.bfloat16)
        return lax.dynamic_update_slice_in_dim(results, blocks, offset, 2)

    stacked = lax.fori_loop(0, head_count, one_head, jnp.zeros((3, length, columns), jnp.bfloat16))
    arrived = from_behind(stacked, "section", -1)
    received = lax.all_to_all(arrived, "mp", split_axis=1, concat_axis=2, tiled=True)
    partial_sums = jnp.sum(received.astype(jnp.float32), axis=1)
    totals = lax.psum(partial_sums, ("dp", "mp"))
    bias_grad = totals / math.sqrt(lax.axis_size("dp") * length)
    return (received[None, None], bias_grad[None])


def solution(mesh):
    return jax.shard_map(
        per_device,
        mesh=mesh,
        in_specs=(
            P("section", "dp", None, "mp"),
            P("section", "dp", None, "mp"),
            P("section", "dp", None, "mp"),
            P("section", "dp", None, "mp"),
            P("section", "dp", None),
        ),
        out_specs=(P("section", "dp", None, "mp", None), P("section", None, None)),
        check_vma=False,
    )
```

profile of v0, /device:TPU:0, one launch (start us, length us, event | category | flops | bytes accessed | tf_op | source)
XLA Modules:
  0.0 304.0 jit_solution(6090517974584673321)
XLA Ops:
  1.3 2.4 broadcast_in_dim.30
  3.8 67.3 %while.14 = (s32[]{:T(128)}, bf16[3,640,1024]{2,1,0:T(8,128)(2,1)}, bf16[640,1024]{1,0:T(8,128)(2,1)}, bf16[640,1024]{1,0:T(8,128)(2,1)}, bf16[640,1024]{1,0:T(8...) while((s32[]{:T(128)}, bf16[3,640,1024]{2,1,0:T(8,128)(2,1)}, ...), condition=%wide.region_4.5_spmd.clone, body=%wide.region_0.4_spmd.clone.sunk | while | flops 534608000 | bytes 16580779 | solution.py:59
  3.8 1.4 fusion.43
  6.8 1.5 multiply_reduce_fusion.2
  8.7 1.3 fusion.47
  12.2 1.4 fusion.43
  15.2 1.5 multiply_reduce_fusion.2
  17.1 1.3 fusion.47
  20.6 1.4 fusion.43
  23.6 1.5 multiply_reduce_fusion.2
  25.5 1.3 fusion.47
  29.0 1.4 fusion.43
  32.0 1.5 multiply_reduce_fusion.2
  37.4 1.4 fusion.43
  40.5 1.5 multiply_reduce_fusion.2
  42.4 1.3 fusion.47
  45.8 1.4 fusion.43
  48.9 1.5 multiply_reduce_fusion.2
  50.8 1.3 fusion.47
  54.2 1.4 fusion.43
  57.3 1.5 multiply_reduce_fusion.2
  59.2 1.3 fusion.47
  62.7 1.4 fusion.43
  65.7 1.5 multiply_reduce_fusion.2
  67.6 1.3 fusion.47
  72.4 88.1 %collective-permute-done = bf16[3,640,1024]{2,1,0:T(8,128)(2,1)S(1)} collective-permute-done((bf16[3,640,1024]{2,1,0:T(8,128)(2,1)}, bf16[3,640,1024]{2,1,0:T(8,128)(2,1)S(1)}, u32[]{:S(2)}, u32[]{:S(2)}) %collective-permute-start) | collective-permute-done | bytes 3932192 | tf_op jit(solution)/shard_map/ppermute | solution.py:13
  160.5 3.4 %copy.10 = bf16[3,640,1024]{2,0,1:T(4,128)(2,1)S(1)} copy(bf16[3,640,1024]{2,1,0:T(8,128)(2,1)S(1)} %collective-permute-done) | data formatting | bytes 7864320 | tf_op jit(solution)/shard_map/ppermute | solution.py:13
  163.9 62.8 %all_to_all.15 = bf16[3,640,1024]{2,0,1:T(4,128)(2,1)S(1)} all-to-all(bf16[3,640,1024]{2,0,1:T(4,128)(2,1)S(1)} %copy.10), channel_id=1, replica_groups=mesh['section'=2,'dp'=4,'mp'=4] {'mp'}, dimensions={1} | all-to-all | bytes 7864320 | tf_op jit(solution)/shard_map/all_to_all | solution.py:61
  226.7 2.0 convert_reduce_fusion
  228.7 5.6 %copy.11 = bf16[3,160,4,1024]{3,2,1,0:T(4,128)(2,1)} copy(bf16[3,160,4,1024]{3,0,1,2:T(4,128)(2,1)S(1)} %bitcast.27) | data formatting | bytes 7864320 | tf_op jit(solution)/shard_map/all_to_all | solution.py:61
  234.3 8.6 %broadcast_in_dim.31 = bf16[1,1,3,160,4096]{4,3,2,1,0:T(8,128)(2,1)} reshape(bf16[3,160,4,1024]{3,2,1,0:T(4,128)(2,1)} %copy.11) | data formatting | bytes 7864320 | tf_op jit(solution)/shard_map/broadcast_in_dim | solution.py:65
  242.9 60.4 %psum.7 = f32[3,4096]{1,0:T(4,128)S(1)} all-reduce(f32[3,4096]{1,0:T(4,128)S(1)} %bitcast.30), channel_id=1, replica_groups=mesh['section'=2,'dp'=4,'mp'=4] {'dp','mp'}, use_global_device_ids=true, to_apply=%region_6.7 | all-reduce | flops 12288 | bytes 98304 | tf_op jit(solution)/shard_map/psum | solution.py:63
  (46 shorter events, 37.1 us)
Async XLA Ops:
  71.1 89.4 %collective-permute-start = (bf16[3,640,1024]{2,1,0:T(8,128)(2,1)}, bf16[3,640,1024]{2,1,0:T(8,128)(2,1)S(1)}, u32[]{:S(2)}, u32[]{:S(2)}) collective-permute-start(bf16[3,640,1024]{2,1,0:T(8,128)(2,1)} %get-tuple-element.126), channel_id=1, source_target_pairs={{16,0},{17,1},{18,2},{19,3},{20,4},{21,5},{22,6},{23,7},{24,8},{25... | collective-permute-start | bytes 11796488 | tf_op jit(solution)/shard_map/ppermute | solution.py:13
where the time goes:
time: 305 us; the launch traced here: 304 us
  blocking collectives  123 us (40%)
  waiting for transfers between devices  88.1 us (29%)
  matrix products  54.9 us (18%)
  local copies, waits for them, and re-layouts  20.6 us (7%)
  other arithmetic  14.9 us (5%)
    ppermute x1, waiting for transfers between devices, from_behind(): lax.ppermute(value, axis, [(source, source + steps) for source in range(i...  88.1 us
    all_to_all x1, blocking collectives, per_device(): lax.all_to_all(arrived, 'mp', split_axis=1, concat_axis=2, tiled=True)  62.8 us
    psum x1, blocking collectives, per_device(): totals = lax.psum(partial_sums, ('dp', 'mp'))  60.4 us
    dot_general x8, matrix products, one_head(): jnp.einsum('qd,kd->qk', grad_part, value_part, preferred_element_type=jnp...  11.8 us
    dot_general x8, matrix products, one_head(): jnp.einsum('qd,kd->qk', query_part, key_part, preferred_element_type=jnp....  11.5 us
    dot_general x8, matrix products, one_head(): jnp.einsum('qk,kd->qd', grad_scores, key_part, preferred_element_type=jnp...  10.6 us
    dot_general x8, matrix products, one_head(): jnp.einsum('qk,qd->kd', attn_low, grad_part, preferred_element_type=jnp.f...  10.5 us
    dot_general x8, matrix products, one_head(): jnp.einsum('qk,qd->kd', grad_scores, query_part, preferred_element_type=j...  10.4 us
  transfers between devices with their start and end apart: 1, of which 1 were waited for; matrix products, arithmetic and copies ran while one was open for 0% of the time, Pallas kernels for 0%

commit v1 on v0

--- a/solution.py
+++ b/solution.py
@@ -58,7 +58,9 @@
 
     stacked = lax.fori_loop(0, head_count, one_head, jnp.zeros((3, length, columns), jnp.bfloat16))
     arrived = from_behind(stacked, "section", -1)
-    received = lax.all_to_all(arrived, "mp", split_axis=1, concat_axis=2, tiled=True)
+    pieces = jnp.split(arrived, lax.axis_size("mp"), axis=1)
+    incoming = lax.all_to_all(jnp.stack(pieces), "mp", 0, 0)
+    received = jnp.concatenate(incoming, axis=2)
     partial_sums = jnp.sum(received.astype(jnp.float32), axis=1)
     totals = lax.psum(partial_sums, ("dp", "mp"))
     bias_grad = totals / math.sqrt(lax.axis_size("dp") * length)

time: 305 us -> 290 us (0.951)
  blocking collectives: 123 us -> 109 us
    all_to_all x1, blocking collectives: 62.8 us -> 48.8 us  [per_device(): incoming = lax.all_to_all(jnp.stack(pieces), 'mp', 0, 0)]
    another operation x0 -> x2, local copies, waits for them, and re-layouts: none -> 9.01 us  [the longest x1 8.6 us: per_device(): return (received[None, None], bias_grad[None])]
    broadcast_in_dim x2 -> x1, local copies, waits for them, and re-layouts: 9.26 us -> 0.65 us  [per_device(): return (received[None, None], bias_grad[None])]
    reshape x0 -> x1, local copies, waits for them, and re-layouts: none -> 7.02 us  [per_device(): received = jnp.concatenate(incoming, axis=2)]
    all_to_all x1 -> x0, local copies, waits for them, and re-layouts: 5.59 us -> none  [per_device(): lax.all_to_all(arrived, 'mp', split_axis=1, concat_axis=2, tiled=True)]
    ppermute x1 -> x0, local copies, waits for them, and re-layouts: 3.37 us -> none  [from_behind(): lax.ppermute(value, axis, [(source, source + steps) for source in range(i...]
where the time goes in v1:
time: 290 us; the launch traced here: 289 us
  blocking collectives  109 us (38%)
  waiting for transfers between devices  88.1 us (30%)
  matrix products  54.9 us (19%)
  local copies, waits for them, and re-layouts  20.2 us (7%)
  other arithmetic  14.3 us (5%)
    ppermute x1, waiting for transfers between devices, from_behind(): lax.ppermute(value, axis, [(source, source + steps) for source in range(i...  88.1 us
    psum x1, blocking collectives, per_device(): totals = lax.psum(partial_sums, ('dp', 'mp'))  60.5 us
    all_to_all x1, blocking collectives, per_device(): incoming = lax.all_to_all(jnp.stack(pieces), 'mp', 0, 0)  48.8 us
    dot_general x8, matrix products, one_head(): jnp.einsum('qd,kd->qk', grad_part, value_part, preferred_element_type=jnp...  11.8 us
    dot_general x8, matrix products, one_head(): jnp.einsum('qd,kd->qk', query_part, key_part, preferred_element_type=jnp....  11.5 us
    dot_general x8, matrix products, one_head(): jnp.einsum('qk,kd->qd', grad_scores, key_part, preferred_element_type=jnp...  10.6 us
    dot_general x8, matrix products, one_head(): jnp.einsum('qk,qd->kd', attn_low, grad_part, preferred_element_type=jnp.f...  10.5 us
    dot_general x8, matrix products, one_head(): jnp.einsum('qk,qd->kd', grad_scores, query_part, preferred_element_type=j...  10.4 us
  transfers between devices with their start and end apart: 1, of which 1 were waited for; matrix products, arithmetic and copies ran while one was open for 0% of the time, Pallas kernels for 0%

profile of v1, /device:TPU:0, one launch (start us, length us, event | category | flops | bytes accessed | tf_op | source)
XLA Modules:
  0.0 289.0 jit_solution(3344130509925505434)
XLA Ops:
  1.3 2.4 broadcast_in_dim.27
  3.8 67.3 %while.14 = (s32[]{:T(128)}, bf16[3,640,1024]{2,1,0:T(8,128)(2,1)}, bf16[640,1024]{1,0:T(8,128)(2,1)}, bf16[640,1024]{1,0:T(8,128)(2,1)}, bf16[640,1024]{1,0:T(8...) while((s32[]{:T(128)}, bf16[3,640,1024]{2,1,0:T(8,128)(2,1)}, ...), condition=%wide.region_4.5_spmd.clone, body=%wide.region_0.4_spmd.clone.sunk | while | flops 534608000 | bytes 16580779 | solution.py:59
  3.8 1.4 fusion.43
  6.8 1.5 multiply_reduce_fusion.2
  8.7 1.3 fusion.47
  12.2 1.4 fusion.43
  15.2 1.5 multiply_reduce_fusion.2
  17.1 1.3 fusion.47
  20.6 1.4 fusion.43
  23.6 1.5 multiply_reduce_fusion.2
  25.5 1.3 fusion.47
  29.0 1.4 fusion.43
  32.0 1.5 multiply_reduce_fusion.2
  33.9 1.3 fusion.47
  37.4 1.4 fusion.43
  39.1 1.3 fusion.45
  40.4 1.5 multiply_reduce_fusion.2
  42.4 1.3 fusion.47
  45.8 1.4 fusion.43
  48.9 1.5 multiply_reduce_fusion.2
  50.8 1.3 fusion.47
  54.2 1.4 fusion.43
  57.3 1.5 multiply_reduce_fusion.2
  59.2 1.3 fusion.47
  62.7 1.4 fusion.43
  65.7 1.5 multiply_reduce_fusion.2
  67.6 1.3 fusion.47
  72.4 88.1 %collective-permute-done = bf16[3,640,1024]{2,1,0:T(8,128)(2,1)S(1)} collective-permute-done((bf16[3,640,1024]{2,1,0:T(8,128)(2,1)}, bf16[3,640,1024]{2,1,0:T(8,128)(2,1)S(1)}, u32[]{:S(2)}, u32[]{:S(2)}) %collective-permute-start) | collective-permute-done | bytes 3932192 | tf_op jit(solution)/shard_map/ppermute | solution.py:13
  161.4 48.8 %all_to_all.5 = bf16[4,3,160,1024]{3,2,1,0:T(8,128)(2,1)S(1)} all-to-all(bf16[4,3,160,1024]{3,2,1,0:T(8,128)(2,1)S(1)} %pad_maximum_fusion), channel_id=1, replica_groups=mesh['section'=2,'dp'=4,'mp'=4] {'mp'}, dimensions={0} | all-to-all | bytes 7864320 | tf_op jit(solution)/shard_map/all_to_all | solution.py:62
  212.1 60.5 %psum.7 = f32[3,4096]{1,0:T(4,128)S(1)} all-reduce(f32[3,4096]{1,0:T(4,128)S(1)} %bitcast.36), channel_id=1, replica_groups=mesh['section'=2,'dp'=4,'mp'=4] {'dp','mp'}, use_global_device_ids=true, to_apply=%region_6.7 | all-reduce | flops 12288 | bytes 98304 | tf_op jit(solution)/shard_map/psum | solution.py:65
  273.3 7.0 %copy.8 = bf16[3,160,4,1024]{3,2,1,0:T(4,128)(2,1)} copy(bf16[3,160,4,1024]{3,1,0,2:T(8,128)(2,1)} %bitcast.33) | data formatting | bytes 7864320 | tf_op jit(solution)/shard_map/reshape | solution.py:63
  280.4 8.6 %broadcast_in_dim_reshape.3 = bf16[1,1,3,160,4096]{4,3,2,1,0:T(8,128)(2,1)} reshape(bf16[3,160,4,1024]{3,2,1,0:T(4,128)(2,1)} %copy.8) | data formatting | bytes 7864320 | tf_op jit(solution)/shard_map/broadcast_in_dim;reshape | solution.py:67
  (49 shorter events, 37.3 us)
Async XLA Ops:
  71.1 89.4 %collective-permute-start = (bf16[3,640,1024]{2,1,0:T(8,128)(2,1)}, bf16[3,640,1024]{2,1,0:T(8,128)(2,1)S(1)}, u32[]{:S(2)}, u32[]{:S(2)}) collective-permute-start(bf16[3,640,1024]{2,1,0:T(8,128)(2,1)} %get-tuple-element.126), channel_id=1, source_target_pairs={{16,0},{17,1},{18,2},{19,3},{20,4},{21,5},{22,6},{23,7},{24,8},{25... | collective-permute-start | bytes 11796488 | tf_op jit(solution)/shard_map/ppermute | solution.py:13
  210.2 1.9 copy-start

commit v2 on v0

--- a/solution.py
+++ b/solution.py
@@ -60,7 +60,11 @@
     arrived = from_behind(stacked, "section", -1)
     received = lax.all_to_all(arrived, "mp", split_axis=1, concat_axis=2, tiled=True)
     partial_sums = jnp.sum(received.astype(jnp.float32), axis=1)
-    totals = lax.psum(partial_sums, ("dp", "mp"))
+
+    def cover_members_all(matrix):
+        return lax.all_gather(matrix, ("dp", "mp")).sum(axis=0)
+
+    totals = cover_members_all(partial_sums)
     bias_grad = totals / math.sqrt(lax.axis_size("dp") * length)
     return (received[None, None], bias_grad[None])
 

time: 305 us -> 268 us (0.88)
  blocking collectives: 123 us -> 86.3 us
    psum x1 -> x0, blocking collectives: 60.4 us -> none  [per_device(): totals = lax.psum(partial_sums, ('dp', 'mp'))]
    all_gather x0 -> x1, blocking collectives: none -> 23.5 us  [cover_members_all(): return lax.all_gather(matrix, ('dp', 'mp')).sum(axis=0)]
    broadcast_in_dim x2 -> x1, local copies, waits for them, and re-layouts: 9.26 us -> 8.6 us  [per_device(): return (received[None, None], bias_grad[None])]
where the time goes in v2:
time: 268 us; the launch traced here: 267 us
  waiting for transfers between devices  88.1 us (33%)
  blocking collectives  86.3 us (32%)
  matrix products  54.9 us (20%)
  local copies, waits for them, and re-layouts  20.6 us (8%)
  other arithmetic  15 us (6%)
    ppermute x1, waiting for transfers between devices, from_behind(): lax.ppermute(value, axis, [(source, source + steps) for source in range(i...  88.1 us
    all_to_all x1, blocking collectives, per_device(): lax.all_to_all(arrived, 'mp', split_axis=1, concat_axis=2, tiled=True)  62.8 us
    all_gather x1, blocking collectives, cover_members_all(): return lax.all_gather(matrix, ('dp', 'mp')).sum(axis=0)  23.5 us
    dot_general x8, matrix products, one_head(): jnp.einsum('qd,kd->qk', grad_part, value_part, preferred_element_type=jnp...  11.8 us
    dot_general x8, matrix products, one_head(): jnp.einsum('qd,kd->qk', query_part, key_part, preferred_element_type=jnp....  11.5 us
    dot_general x8, matrix products, one_head(): jnp.einsum('qk,kd->qd', grad_scores, key_part, preferred_element_type=jnp...  10.6 us
    dot_general x8, matrix products, one_head(): jnp.einsum('qk,qd->kd', attn_low, grad_part, preferred_element_type=jnp.f...  10.5 us
    dot_general x8, matrix products, one_head(): jnp.einsum('qk,qd->kd', grad_scores, query_part, preferred_element_type=j...  10.4 us
  transfers between devices with their start and end apart: 1, of which 1 were waited for; matrix products, arithmetic and copies ran while one was open for 0% of the time, Pallas kernels for 0%

profile of v2, /device:TPU:0, one launch (start us, length us, event | category | flops | bytes accessed | tf_op | source)
XLA Modules:
  0.0 267.3 jit_solution(12472266278593307780)
XLA Ops:
  1.3 2.4 broadcast_in_dim.28
  3.8 67.3 %while.14 = (s32[]{:T(128)}, bf16[3,640,1024]{2,1,0:T(8,128)(2,1)}, bf16[640,1024]{1,0:T(8,128)(2,1)}, bf16[640,1024]{1,0:T(8,128)(2,1)}, bf16[640,1024]{1,0:T(8...) while((s32[]{:T(128)}, bf16[3,640,1024]{2,1,0:T(8,128)(2,1)}, ...), condition=%wide.region_4.5_spmd.clone, body=%wide.region_0.4_spmd.clone.sunk | while | flops 534608000 | bytes 16580779 | solution.py:59
  3.8 1.4 fusion.43
  6.8 1.5 multiply_reduce_fusion.2
  8.7 1.3 fusion.47
  12.2 1.4 fusion.43
  15.2 1.5 multiply_reduce_fusion.2
  17.1 1.3 fusion.47
  20.6 1.4 fusion.43
  23.6 1.5 multiply_reduce_fusion.2
  25.5 1.3 fusion.47
  29.0 1.4 fusion.43
  32.0 1.5 multiply_reduce_fusion.2
  37.4 1.4 fusion.43
  40.5 1.5 multiply_reduce_fusion.2
  42.4 1.3 fusion.47
  45.8 1.4 fusion.43
  48.9 1.5 multiply_reduce_fusion.2
  50.8 1.3 fusion.47
  54.2 1.4 fusion.43
  57.3 1.5 multiply_reduce_fusion.2
  59.2 1.3 fusion.47
  62.7 1.4 fusion.43
  65.7 1.5 multiply_reduce_fusion.2
  67.6 1.3 fusion.47
  72.4 88.1 %collective-permute-done = bf16[3,640,1024]{2,1,0:T(8,128)(2,1)S(1)} collective-permute-done((bf16[3,640,1024]{2,1,0:T(8,128)(2,1)}, bf16[3,640,1024]{2,1,0:T(8,128)(2,1)S(1)}, u32[]{:S(2)}, u32[]{:S(2)}) %collective-permute-start) | collective-permute-done | bytes 3932192 | tf_op jit(solution)/shard_map/ppermute | solution.py:13
  160.5 3.4 %copy.11 = bf16[3,640,1024]{2,0,1:T(4,128)(2,1)S(1)} copy(bf16[3,640,1024]{2,1,0:T(8,128)(2,1)S(1)} %collective-permute-done) | data formatting | bytes 7864320 | tf_op jit(solution)/shard_map/ppermute | solution.py:13
  163.9 62.8 %all_to_all.15 = bf16[3,640,1024]{2,0,1:T(4,128)(2,1)S(1)} all-to-all(bf16[3,640,1024]{2,0,1:T(4,128)(2,1)S(1)} %copy.11), channel_id=1, replica_groups=mesh['section'=2,'dp'=4,'mp'=4] {'mp'}, dimensions={1} | all-to-all | bytes 7864320 | tf_op jit(solution)/shard_map/all_to_all | solution.py:61
  226.7 2.0 convert_reduce_fusion
  228.7 5.6 %copy.12 = bf16[3,160,4,1024]{3,2,1,0:T(4,128)(2,1)} copy(bf16[3,160,4,1024]{3,0,1,2:T(4,128)(2,1)S(1)} %bitcast.27) | data formatting | bytes 7864320 | tf_op jit(solution)/shard_map/all_to_all | solution.py:61
  234.3 8.6 %broadcast_in_dim.29 = bf16[1,1,3,160,4096]{4,3,2,1,0:T(8,128)(2,1)} reshape(bf16[3,160,4,1024]{3,2,1,0:T(4,128)(2,1)} %copy.12) | data formatting | bytes 7864320 | tf_op jit(solution)/shard_map/broadcast_in_dim | solution.py:69
  242.9 23.5 %all_gather.7 = f32[16,3,4096]{2,1,0:T(4,128)S(1)} all-gather(f32[1,3,4096]{2,1,0:T(4,128)S(1)} %bitcast.30), channel_id=1, replica_groups=mesh['section'=2,'dp'=4,'mp'=4] {'dp','mp'}, dimensions={0}, use_global_device_ids=true | all-gather | bytes 835584 | tf_op jit(solution)/shard_map/all_gather | solution.py:65
  (47 shorter events, 37.2 us)
Async XLA Ops:
  71.1 89.4 %collective-permute-start = (bf16[3,640,1024]{2,1,0:T(8,128)(2,1)}, bf16[3,640,1024]{2,1,0:T(8,128)(2,1)S(1)}, u32[]{:S(2)}, u32[]{:S(2)}) collective-permute-start(bf16[3,640,1024]{2,1,0:T(8,128)(2,1)} %get-tuple-element.126), channel_id=1, source_target_pairs={{16,0},{17,1},{18,2},{19,3},{20,4},{21,5},{22,6},{23,7},{24,8},{25... | collective-permute-start | bytes 11796488 | tf_op jit(solution)/shard_map/ppermute | solution.py:13
